TPU v7x, 256 devices: a whole 4x4x8 slice. The times are simulated.
256 devices in a mesh: ctx: 32 (over z, y_hi, core), head: 8 (over x, y_lo).
Axes of the slice: x: 4, y: 4 (y_hi: 2, y_lo: 2; y = y_hi * 2 + y_lo), z: 8, core: 2. Of those that a mesh axis runs over, the one named last changes fastest.
Arguments:
- doc_lengths: int32 [16], replicated, may hold values from 1 to 4352, 8192 in all
- queries: bfloat16 [2, 8192, 16384], P(None, 'ctx', 'head'), may hold values from -120 to 120
- rotated_key_rows: bfloat16 [2, 8192, 1024], P(None, ('ctx', 'head')), may hold values from -6 to 6
- value_row_matrix: bfloat16 [2, 8192, 1024], P(None, ('ctx', 'head')), may hold values from -6 to 6
Outputs:
- attended: bfloat16 [2, 8192, 16384], P(None, 'ctx', 'head')
All inputs are finite; a program needn't handle non-finite values.
Results may differ from a plain program's by a relative error of at most 0.003.
Values may be sent and summed in bfloat16 or wider, within the bound.
No kernel may reach another device: no remote copies, remote signals or barrier semaphores. Data moves between devices by JAX's collectives and lax.ppermute only.
A program may use at most 64 MiB of HBM per device.

v0:
```python
import functools

import jax
import jax.numpy as jnp
from jax import lax
from jax.experimental import pallas as pl
from jax.experimental.pallas import tpu as pltpu
from jax.sharding import PartitionSpec as P

HEAD_SIZE = 128
LONGEST = 4352
NEG_FILL = -1e30

KEY_TILE = 512
STAT_LANES = 128
LOG2E = 1.4426950408889634


def attend_kernel(meta_ref, lo_ref, hi_ref, q_ref, k_ref, v_ref, o_ref,
                  peak_sc, total_sc, accum_sc, *, key_tile, steps, scale, heads):
    step = pl.program_id(1)
    block = meta_ref[0] + step
    key_start = block * key_tile

    @pl.when(step == 0)
    def _():
        peak_sc[...] = jnp.full(peak_sc.shape, NEG_FILL, jnp.float32)
        total_sc[...] = jnp.zeros(total_sc.shape, jnp.float32)
        accum_sc[...] = jnp.zeros(accum_sc.shape, jnp.float32)

    live = block <= meta_ref[1]
    inner = (key_start >= meta_ref[2]) & (key_start + key_tile - 1 <= meta_ref[3])
    reps = key_tile // STAT_LANES

    def update(masked):
        keys = k_ref[0]
        values = v_ref[0]
        if masked:
            key_pos = key_start + lax.broadcasted_iota(jnp.int32, (1, key_tile), 1)
            allowed = (key_pos >= lo_ref[...]) & (key_pos <= hi_ref[...])
        for h in range(heads):
            cols = slice(h * HEAD_SIZE, (h + 1) * HEAD_SIZE)
            scores = lax.dot_general(
                q_ref[0, :, cols], keys, (((1,), (1,)), ((), ())),
                preferred_element_type=jnp.float32)
            if masked:
                scores = jnp.where(allowed, scores, NEG_FILL)
            peak_old = peak_sc[h]
            peak_new = jnp.maximum(peak_old, jnp.max(scores, axis=-1, keepdims=True))
            shift = peak_new * scale
            probs = jnp.exp2(scores * scale - jnp.tile(shift, (1, reps)))
            if masked:
                probs = jnp.where(allowed, probs, 0.0)
            factor = jnp.exp2(peak_old * scale - shift)
            total_sc[h] = total_sc[h] * factor + jnp.sum(probs, axis=-1, keepdims=True)
            accum_sc[h] = accum_sc[h] * factor + lax.dot_general(
                probs.astype(jnp.bfloat16), values, (((1,), (0,)), ((), ())),
                preferred_element_type=jnp.float32)
            peak_sc[h] = peak_new

    @pl.when(live & inner)
    def _():
        update(False)

    @pl.when(live & jnp.logical_not(inner))
    def _():
        update(True)

    @pl.when(step == steps - 1)
    def _():
        for h in range(heads):
            cols = slice(h * HEAD_SIZE, (h + 1) * HEAD_SIZE)
            o_ref[0, :, cols] = (accum_sc[h] / total_sc[h]).astype(o_ref.dtype)


def attend(queries, kv, meta, lo, hi):
    models, query_count, feature_width = queries.shape
    heads = feature_width // HEAD_SIZE
    key_count = kv.shape[1]
    key_tile = min(KEY_TILE, key_count)
    steps = min(key_count // key_tile, (LONGEST + query_count - 2) // key_tile + 2)

    def key_map(b, j, meta_ref):
        return (b, jnp.minimum(meta_ref[0] + j, meta_ref[1]), 0)

    def value_map(b, j, meta_ref):
        return (b, jnp.minimum(meta_ref[0] + j, meta_ref[1]), 1)

    kernel = functools.partial(
        attend_kernel, key_tile=key_tile, steps=steps,
        scale=HEAD_SIZE ** (-0.5) * LOG2E, heads=heads)
    return pl.pallas_call(
        kernel,
        out_shape=jax.ShapeDtypeStruct(queries.shape, jnp.bfloat16),
        grid_spec=pltpu.PrefetchScalarGridSpec(
            num_scalar_prefetch=1,
            grid=(models, steps),
            in_specs=[
                pl.BlockSpec((query_count, 1), lambda b, j, m: (0, 0)),
                pl.BlockSpec((query_count, 1), lambda b, j, m: (0, 0)),
                pl.BlockSpec((1, query_count, feature_width), lambda b, j, m: (b, 0, 0)),
                pl.BlockSpec((1, key_tile, HEAD_SIZE), key_map),
                pl.BlockSpec((1, key_tile, HEAD_SIZE), value_map),
            ],
            out_specs=pl.BlockSpec((1, query_count, feature_width), lambda b, j, m: (b, 0, 0)),
            scratch_shapes=[
                pltpu.VMEM((heads, query_count, STAT_LANES), jnp.float32),
                pltpu.VMEM((heads, query_count, STAT_LANES), jnp.float32),
                pltpu.VMEM((heads, query_count, HEAD_SIZE), jnp.float32),
            ],
        ),
        compiler_params=pltpu.CompilerParams(dimension_semantics=("arbitrary", "arbitrary")),
    )(meta, lo, hi, queries, kv, kv)


def shards(doc_lengths, queries, rotated_key_rows, value_row_matrix):
    models, query_count, feature_width = queries.shape
    kv_heads = rotated_key_rows.shape[2] // HEAD_SIZE
    head_groups = lax.axis_size("head")
    assert kv_heads == head_groups
    local_rows = rotated_key_rows.shape[1]
    paired = jnp.stack(
        [
            rotated_key_rows.reshape(models, local_rows, kv_heads, HEAD_SIZE),
            value_row_matrix.reshape(models, local_rows, kv_heads, HEAD_SIZE),
        ],
        axis=3,
    ).reshape(models, local_rows, kv_heads * 2 * HEAD_SIZE)
    local_kv = lax.all_to_all(paired, "head", split_axis=2, concat_axis=1, tiled=True)

    doc_ends = jnp.cumsum(doc_lengths).astype(jnp.int32)
    query_start = lax.axis_index("ctx") * query_count
    query_pos = query_start + jnp.arange(query_count, dtype=jnp.int32)
    query_lo = jnp.max(
        jnp.where(doc_ends[None, :] <= query_pos[:, None], doc_ends[None, :], 0), axis=1)
    key_tile = min(KEY_TILE, query_count * lax.axis_size("ctx"))
    meta = jnp.stack([
        query_lo[0] // key_tile,
        query_pos[-1] // key_tile,
        query_lo[-1],
        query_pos[0],
    ]).astype(jnp.int32)
    lo = query_lo.reshape(query_count, 1)
    hi = query_pos.reshape(query_count, 1)

    kv = lax.all_gather(local_kv, "ctx", axis=1, tiled=True)
    return attend(queries, kv, meta, lo, hi)


def solution(mesh):
    placed = (
        P(),
        P(None, "ctx", "head"),
        P(None, ("ctx", "head"), None),
        P(None, ("ctx", "head"), None),
    )
    return jax.shard_map(
        shards, mesh=mesh, in_specs=placed, out_specs=P(None, "ctx", "head"), check_vma=False
    )
```

profile of v0, /device:TPU:193, one launch (start us, length us, event | category | flops | bytes accessed | tf_op | source)
XLA Modules:
  0.0 239.5 jit_solution(3843693801899864194)
XLA Ops:
  6.5 0.0 all-gather.2.cloned.1.call-start
  6.5 1.0 stack_reshape.8
  7.5 1.0 stack_reshape.9
  8.5 0.6 pad_maximum_fusion
  9.2 0.9 copy.25
  10.0 0.0 copy-start
  10.0 1.0 reshape.44
  11.0 10.8 %all_to_all.18 = bf16[8,2,8192]{2,1,0:T(2,128)(2,1)S(1)} all-to-all(bf16[8,2,8192]{2,1,0:T(2,128)(2,1)S(1)} %reshape.44), channel_id=1, replica_groups=mesh['ctx'=32,'head'=8] {'head'}, dimensions={0} | all-to-all | bytes 524288 | tf_op jit(solution)/shard_map/all_to_all | solution.py:129
  21.7 0.5 reshape.45
  22.2 1.8 copy.27
  24.0 0.0 all-gather.2.cloned.1.call-update
  24.1 0.0 copy-done
  24.1 0.1 copy.18
  24.2 0.1 reduce
  24.3 0.1 select_reduce_fusion
  24.4 0.7 fusion
  29.9 0.8 copy.24.lo_ref
  30.7 1.9 pad_add_fusion.meta_ref
  32.6 0.6 iota_add_fusion.hi_ref
  33.2 90.8 %all-gather.2.cloned.1.call-done.k_ref.v_ref = bf16[2,8192,256]{2,1,0:T(8,128)(2,1)} async-done(((bf16[2,256,256]{2,1,0:T(8,128)(2,1)}), bf16[2,8192,256]{2,1,0:T(8,128)(2,1)}) %all-gather.2.cloned.1.call-update) | async-done | bytes 8388624 | tf_op jit(solution)/shard_map/all_gather | solution.py:146
  124.0 108.7 %shard_map.46 = bf16[2,256,2048]{2,1,0:T(8,128)(2,1)} custom-call(s32[4]{0:T(128)} %pad_add_fusion.meta_ref, s32[256,1]{1,0:T(8,128)} %copy.24.lo_ref, s32[256,1]{1,0:T(8,128)} %iota_add_fusion.hi_ref, bf16[2,256,2048]{2,1,0:T(8,128)(2,1)} %q_ref.1, bf16[2,8192,256]{2,1,0:T(8,128)(2,1)} %all-gather.2.cloned.1.call-done.k_ref.v_ref, ...), custom_call_target="tpu_custom_call" | custom-call | tf_op jit(solution)/shard_map/pallas_call | solution.py:92
  (2 shorter events, 0.0 us)
Async XLA Ops:
  6.5 117.5 %all-gather.2.cloned.1.call-start = ((), (), s32[]{:S(2)}) async-start(), calls=%async_computation.1 | async-start | bytes 8650752 | tf_op jit(solution)/shard_map/all_gather | solution.py:146
  10.0 14.0 %copy-start = (s32[16]{0:T(128)S(1)}, s32[16]{0:T(128)}, u32[]{:S(2)}) copy-start(s32[16]{0:T(128)} %param.4) | copy-start | bytes 196
Sparse Core Ops, SparseCore 0:
  24.2 99.8 all-gather.1
where the time goes:
time: 244 us; the launch traced here: 240 us
  Pallas kernels  109 us (45%)
  waiting for transfers between devices  90.8 us (37%)
  between operations  18.3 us (8%)
  blocking collectives  10.8 us (4%)
  local copies, waits for them, and re-layouts  7.62 us (3%)
  other arithmetic  3.4 us (1%)
    pallas_call x1, Pallas kernels, attend(): pl.pallas_call(kernel, out_shape=jax.ShapeDtypeStruct(queries.shape, jnp....  109 us
    all_gather x1, waiting for transfers between devices, shards(): kv = lax.all_gather(local_kv, 'ctx', axis=1, tiled=True)  90.8 us
    all_to_all x1, blocking collectives, shards(): lax.all_to_all(paired, 'head', split_axis=2, concat_axis=1, tiled=True)  10.8 us
  transfers between devices with their start and end apart: 1, of which 1 were waited for; matrix products, arithmetic and copies ran while one was open for 2% of the time, Pallas kernels for 0%

commit v1 on v0

v1 whole, which is shorter than its diff:
```python
import functools

import jax
import jax.numpy as jnp
from jax import lax
from jax.experimental import pallas as pl
from jax.experimental.pallas import tpu as pltpu
from jax.sharding import PartitionSpec as P


HEAD_SIZE = 128
LONGEST = 4352
NEG_FILL = -1e30

KEY_TILE = 512
STAT_LANES = 128
LOG2E = 1.4426950408889634
NEAR_BLOCKS = 3


def attend_kernel(meta_ref, lo_ref, hi_ref, q_ref, k_ref, v_ref, *rest,
                  key_tile, steps, scale, heads, resume, finish):
    if resume:
        peak_in, total_in, accum_in = rest[:3]
        rest = rest[3:]
    if finish:
        o_ref, peak_sc, total_sc, accum_sc = rest
    else:
        peak_out, total_out, accum_out, peak_sc, total_sc, accum_sc = rest
    step = pl.program_id(1)
    block = meta_ref[0] + step
    key_start = meta_ref[4] + block * key_tile

    @pl.when(step == 0)
    def _():
        if resume:
            peak_sc[...] = peak_in[0]
            total_sc[...] = total_in[0]
            accum_sc[...] = accum_in[0]
        else:
            peak_sc[...] = jnp.full(peak_sc.shape, NEG_FILL, jnp.float32)
            total_sc[...] = jnp.zeros(total_sc.shape, jnp.float32)
            accum_sc[...] = jnp.zeros(accum_sc.shape, jnp.float32)

    live = block <= meta_ref[1]
    inner = (key_start >= meta_ref[2]) & (key_start + key_tile - 1 <= meta_ref[3])
    reps = key_tile // STAT_LANES

    def update(masked):
        keys = k_ref[0]
        values = v_ref[0]
        if masked:
            key_pos = key_start + lax.broadcasted_iota(jnp.int32, (1, key_tile), 1)
            allowed = (key_pos >= lo_ref[...]) & (key_pos <= hi_ref[...])
        for h in range(heads):
            cols = slice(h * HEAD_SIZE, (h + 1) * HEAD_SIZE)
            scores = lax.dot_general(
                q_ref[0, :, cols], keys, (((1,), (1,)), ((), ())),
                preferred_element_type=jnp.float32)
            if masked:
                scores = jnp.where(allowed, scores, NEG_FILL)
            peak_old = peak_sc[h]
            peak_new = jnp.maximum(peak_old, jnp.max(scores, axis=-1, keepdims=True))
            shift = peak_new * scale
            probs = jnp.exp2(scores * scale - jnp.tile(shift, (1, reps)))
            if masked:
                probs = jnp.where(allowed, probs, 0.0)
            factor = jnp.exp2(peak_old * scale - shift)
            total_sc[h] = total_sc[h] * factor + jnp.sum(probs, axis=-1, keepdims=True)
            accum_sc[h] = accum_sc[h] * factor + lax.dot_general(
                probs.astype(jnp.bfloat16), values, (((1,), (0,)), ((), ())),
                preferred_element_type=jnp.float32)
            peak_sc[h] = peak_new

    @pl.when(live & inner)
    def _():
        update(False)

    @pl.when(live & jnp.logical_not(inner))
    def _():
        update(True)

    @pl.when(step == steps - 1)
    def _():
        if finish:
            for h in range(heads):
                cols = slice(h * HEAD_SIZE, (h + 1) * HEAD_SIZE)
                o_ref[0, :, cols] = (accum_sc[h] / total_sc[h]).astype(o_ref.dtype)
        else:
            peak_out[0] = peak_sc[...]
            total_out[0] = total_sc[...]
            accum_out[0] = accum_sc[...]


def attend(queries, kv, meta, lo, hi, state, steps_cap):
    models, query_count, feature_width = queries.shape
    heads = feature_width // HEAD_SIZE
    key_count = kv.shape[1]
    key_tile = min(KEY_TILE, key_count)
    steps = min(key_count // key_tile, steps_cap)
    resume = state is not None
    finish = resume

    def key_map(b, j, meta_ref):
        return (b, jnp.maximum(jnp.minimum(meta_ref[0] + j, meta_ref[1]), 0), 0)

    def value_map(b, j, meta_ref):
        return (b, jnp.maximum(jnp.minimum(meta_ref[0] + j, meta_ref[1]), 0), 1)

    stat_shape = (models, heads, query_count, STAT_LANES)
    stat_spec = pl.BlockSpec((1, heads, query_count, STAT_LANES), lambda b, j, m: (b, 0, 0, 0))
    in_specs = [
        pl.BlockSpec((query_count, 1), lambda b, j, m: (0, 0)),
        pl.BlockSpec((query_count, 1), lambda b, j, m: (0, 0)),
        pl.BlockSpec((1, query_count, feature_width), lambda b, j, m: (b, 0, 0)),
        pl.BlockSpec((1, key_tile, HEAD_SIZE), key_map),
        pl.BlockSpec((1, key_tile, HEAD_SIZE), value_map),
    ]
    operands = [meta, lo, hi, queries, kv, kv]
    if resume:
        in_specs += [stat_spec] * 3
        operands += list(state)
    if finish:
        out_shape = jax.ShapeDtypeStruct(queries.shape, jnp.bfloat16)
        out_specs = pl.BlockSpec((1, query_count, feature_width), lambda b, j, m: (b, 0, 0))
    else:
        out_shape = [jax.ShapeDtypeStruct(stat_shape, jnp.float32)] * 3
        out_specs = [stat_spec] * 3

    kernel = functools.partial(
        attend_kernel, key_tile=key_tile, steps=steps,
        scale=HEAD_SIZE ** (-0.5) * LOG2E, heads=heads, resume=resume, finish=finish)
    return pl.pallas_call(
        kernel,
        out_shape=out_shape,
        grid_spec=pltpu.PrefetchScalarGridSpec(
            num_scalar_prefetch=1,
            grid=(models, steps),
            in_specs=in_specs,
            out_specs=out_specs,
            scratch_shapes=[
                pltpu.VMEM((heads, query_count, STAT_LANES), jnp.float32),
                pltpu.VMEM((heads, query_count, STAT_LANES), jnp.float32),
                pltpu.VMEM((heads, query_count, HEAD_SIZE), jnp.float32),
            ],
        ),
        compiler_params=pltpu.CompilerParams(dimension_semantics=("arbitrary", "arbitrary")),
    )(*operands)


def layer(doc_lengths, queries, rotated_key_rows, value_row_matrix):
    models, query_count, _ = queries.shape
    kv_heads = rotated_key_rows.shape[2] // HEAD_SIZE
    head_groups = lax.axis_size("head")
    assert kv_heads == head_groups
    local_rows = rotated_key_rows.shape[1]
    paired = jnp.stack(
        [
            rotated_key_rows.reshape(models, local_rows, kv_heads, HEAD_SIZE),
            value_row_matrix.reshape(models, local_rows, kv_heads, HEAD_SIZE),
        ],
        axis=3,
    ).reshape(models, local_rows, kv_heads * 2 * HEAD_SIZE)
    local_kv = lax.all_to_all(paired, "head", split_axis=2, concat_axis=1, tiled=True)

    ctx_size = lax.axis_size("ctx")
    near_kv = jnp.concatenate(
        [
            lax.ppermute(local_kv, "ctx", [(i, i + k) for i in range(ctx_size - k)])
            for k in range(NEAR_BLOCKS, 0, -1)
        ]
        + [local_kv],
        axis=1,
    )
    kv = lax.all_gather(local_kv, "ctx", axis=1, tiled=True)

    doc_ends = jnp.cumsum(doc_lengths).astype(jnp.int32)
    query_start = lax.axis_index("ctx") * query_count
    query_pos = query_start + jnp.arange(query_count, dtype=jnp.int32)
    query_lo = jnp.max(
        jnp.where(doc_ends[None, :] <= query_pos[:, None], doc_ends[None, :], 0), axis=1)
    key_tile = min(KEY_TILE, query_count * ctx_size)
    near_start = query_start - NEAR_BLOCKS * query_count
    near_meta = jnp.stack([
        jnp.maximum(query_lo[0] - near_start, 0) // key_tile,
        (query_pos[-1] - near_start) // key_tile,
        query_lo[-1],
        query_pos[0],
        near_start,
    ]).astype(jnp.int32)
    far_hi = jnp.minimum(query_pos, near_start - 1)
    far_meta = jnp.stack([
        query_lo[0] // key_tile,
        jnp.where(near_start > 0, (near_start - 1) // key_tile, -1),
        query_lo[-1],
        far_hi[0],
        0,
    ]).astype(jnp.int32)
    lo = query_lo.reshape(query_count, 1)
    state = attend(queries, near_kv, near_meta, lo, query_pos.reshape(query_count, 1), None,
                   near_kv.shape[1] // key_tile)
    return attend(queries, kv, far_meta, lo, far_hi.reshape(query_count, 1), state,
                  (LONGEST + query_count - 2) // key_tile + 2)


def solution(mesh):
    placed = (
        P(),
        P(None, "ctx", "head"),
        P(None, ("ctx", "head"), None),
        P(None, ("ctx", "head"), None),
    )
    return jax.shard_map(
        layer, mesh=mesh, in_specs=placed, out_specs=P(None, "ctx", "head"), check_vma=False
    )
```

time: 244 us -> 223 us (0.914)
  the two profiles are of different devices: /device:TPU:193 before, /device:TPU:225 now
where the time goes in v1:
time: 223 us; the launch traced here: 222 us
  Pallas kernels  120 us (54%)
  waiting for transfers between devices  47.6 us (21%)
  between operations  17.3 us (8%)
  local copies, waits for them, and re-layouts  12.5 us (6%)
  blocking collectives  10.8 us (5%)
  starting transfers between devices  10 us (4%)
  other arithmetic  4.18 us (2%)
    pallas_call x2, Pallas kernels, attend(): pl.pallas_call(kernel, out_shape=out_shape, grid_spec=pltpu.PrefetchScala...  120 us
    all_gather x1, waiting for transfers between devices, layer(): kv = lax.all_gather(local_kv, 'ctx', axis=1, tiled=True)  44.2 us
    all_to_all x1, blocking collectives, layer(): lax.all_to_all(paired, 'head', split_axis=2, concat_axis=1, tiled=True)  10.8 us
    ppermute x3, starting transfers between devices, layer(): lax.ppermute(local_kv, 'ctx', [(i, i + k) for i in range(ctx_size - k)])  10 us
  transfers between devices with their start and end apart: 4, of which 2 were waited for; matrix products, arithmetic and copies ran while one was open for 4% of the time, Pallas kernels for 13%

profile of v1, /device:TPU:225, one launch (start us, length us, event | category | flops | bytes accessed | tf_op | source)
XLA Modules:
  0.0 222.3 jit_solution(891228197032265626)
XLA Ops:
  6.5 1.0 stack_reshape.8
  7.5 1.0 stack_reshape.9
  8.5 0.6 pad_maximum_fusion.1
  9.2 0.9 copy.28
  10.0 1.0 reshape.49
  11.0 10.8 %all_to_all.18 = bf16[8,2,8192]{2,1,0:T(2,128)(2,1)S(1)} all-to-all(bf16[8,2,8192]{2,1,0:T(2,128)(2,1)S(1)} %reshape.49), channel_id=1, replica_groups=mesh['ctx'=32,'head'=8] {'head'}, dimensions={0} | all-to-all | bytes 524288 | tf_op jit(solution)/shard_map/all_to_all | solution.py:164
  21.7 0.5 reshape.50
  22.2 1.8 copy.30
  24.3 0.6 fusion
  25.0 6.6 %collective-permute-start.2 = (bf16[2,256,256]{2,1,0:T(8,128)(2,1)}, bf16[2,256,256]{2,1,0:T(8,128)(2,1)S(1)}, u32[]{:S(2)}, u32[]{:S(2)}) collective-permute-start(bf16[2,256,256]{2,1,0:T(8,128)(2,1)} %bitcast.20), channel_id=1, source_target_pairs={{0,8},{8,16},{16,24},{24,32},{32,40},{40,48},{48,56},{56,64},{64,7... | collective-permute-start | bytes 786440 | tf_op jit(solution)/shard_map/ppermute | solution.py:169
  31.7 1.9 collective-permute-start.1
  33.6 1.5 collective-permute-start
  35.1 0.6 fusion.1
  39.5 0.5 slice.19
  40.0 0.8 copy.27.lo_ref
  40.8 1.9 stack.31.meta_ref
  42.8 1.8 stack.26.meta_ref
  44.6 0.7 broadcast_minimum_fusion.hi_ref
  45.3 0.7 iota_add_fusion.hi_ref
  46.0 3.4 %collective-permute-done = bf16[2,256,256]{2,1,0:T(8,128)(2,1)S(1)} collective-permute-done((bf16[2,256,256]{2,1,0:T(8,128)(2,1)}, bf16[2,256,256]{2,1,0:T(8,128)(2,1)S(1)}, u32[]{:S(2)}, u32[]{:S(2)}) %collective-permute-start) | collective-permute-done | bytes 262176 | tf_op jit(solution)/shard_map/ppermute | solution.py:169
  49.3 2.0 pad_maximum_fusion.k_ref.v_ref
  51.3 29.2 %shard_map.46 = (f32[2,16,256,128]{3,2,1,0:T(8,128)}, f32[2,16,256,128]{3,2,1,0:T(8,128)}, f32[2,16,256,128]{3,2,1,0:T(8,128)}) custom-call(s32[5]{0:T(128)} %stack.31.meta_ref, s32[256,1]{1,0:T(8,128)} %copy.27.lo_ref, s32[256,1]{1,0:T(8,128)} %iota_add_fusion.hi_ref, bf16[2,256,2048]{2,1,0:T(8,128)(2,1)} %q_ref.3, ...), custom_call_target="tpu_custom_call" | custom-call | tf_op jit(solution)/shard_map/pallas_call | solution.py:133
  80.5 44.2 %all-gather.2.cloned.1.call-done.k_ref.v_ref = bf16[2,8192,256]{2,1,0:T(8,128)(2,1)} async-done(((bf16[2,256,256]{2,1,0:T(8,128)(2,1)}), bf16[2,8192,256]{2,1,0:T(8,128)(2,1)}) %all-gather.2.cloned.1.call-update) | async-done | bytes 8388624 | tf_op jit(solution)/shard_map/all_gather | solution.py:175
  124.7 90.8 %shard_map.47 = bf16[2,256,2048]{2,1,0:T(8,128)(2,1)} custom-call(s32[5]{0:T(128)} %stack.26.meta_ref, s32[256,1]{1,0:T(8,128)} %copy.27.lo_ref, s32[256,1]{1,0:T(8,128)} %broadcast_minimum_fusion.hi_ref, bf16[2,256,2048]{2,1,0:T(8,128)(2,1)} %q_ref.3, bf16[2,8192,256]{2,1,0:T(8,128)(2,1)} %all-gather.2.cloned.1.call-done.k_ref.v_ref, ...), custom_call_target="tpu_custom_call" | custom-call | tf_op jit(solution)/shard_map/pallas_call | solution.py:133
  (11 shorter events, 0.4 us)
Async XLA Ops:
  6.5 118.2 %all-gather.2.cloned.1.call-start = ((), (), s32[]{:S(2)}) async-start(), calls=%async_computation.1 | async-start | bytes 8650752 | tf_op jit(solution)/shard_map/all_gather | solution.py:175
  10.0 14.0 %copy-start = (s32[16]{0:T(128)S(1)}, s32[16]{0:T(128)}, u32[]{:S(2)}) copy-start(s32[16]{0:T(128)} %param.4) | copy-start | bytes 196
  25.0 20.9 %collective-permute-start.2 = (bf16[2,256,256]{2,1,0:T(8,128)(2,1)}, bf16[2,256,256]{2,1,0:T(8,128)(2,1)S(1)}, u32[]{:S(2)}, u32[]{:S(2)}) collective-permute-start(bf16[2,256,256]{2,1,0:T(8,128)(2,1)} %bitcast.20), channel_id=1, source_target_pairs={{0,8},{8,16},{16,24},{24,32},{32,40},{40,48},{48,56},{56,64},{64,7... | collective-permute-start | bytes 786440 | tf_op jit(solution)/shard_map/ppermute | solution.py:169
  31.7 14.3 %collective-permute-start.1 = (bf16[2,256,256]{2,1,0:T(8,128)(2,1)}, bf16[2,256,256]{2,1,0:T(8,128)(2,1)S(1)}, u32[]{:S(2)}, u32[]{:S(2)}) collective-permute-start(bf16[2,256,256]{2,1,0:T(8,128)(2,1)} %bitcast.21), channel_id=1, source_target_pairs={{0,16},{8,24},{16,32},{24,40},{32,48},{40,56},{48,64},{56,72},{64,... | collective-permute-start | bytes 786440 | tf_op jit(solution)/shard_map/ppermute | solution.py:169
  33.6 15.7 %collective-permute-start = (bf16[2,256,256]{2,1,0:T(8,128)(2,1)}, bf16[2,256,256]{2,1,0:T(8,128)(2,1)S(1)}, u32[]{:S(2)}, u32[]{:S(2)}) collective-permute-start(bf16[2,256,256]{2,1,0:T(8,128)(2,1)} %bitcast.22), channel_id=1, source_target_pairs={{0,24},{8,32},{16,40},{24,48},{32,56},{40,64},{48,72},{56,80},{64,... | collective-permute-start | bytes 786440 | tf_op jit(solution)/shard_map/ppermute | solution.py:169
Sparse Core Ops, SparseCore 0:
  24.1 100.5 all-gather.1

commit v2 on v1

--- a/solution.py
+++ b/solution.py
@@ -12,10 +12,10 @@
 LONGEST = 4352
 NEG_FILL = -1e30
 
-KEY_TILE = 512
+KEY_TILE = 1024
 STAT_LANES = 128
 LOG2E = 1.4426950408889634
-NEAR_BLOCKS = 3
+NEAR_BLOCKS = 7
 
 
 def attend_kernel(meta_ref, lo_ref, hi_ref, q_ref, k_ref, v_ref, *rest,
@@ -52,8 +52,8 @@
         if masked:
             key_pos = key_start + lax.broadcasted_iota(jnp.int32, (1, key_tile), 1)
             allowed = (key_pos >= lo_ref[...]) & (key_pos <= hi_ref[...])
-        for h in range(heads):
-            cols = slice(h * HEAD_SIZE, (h + 1) * HEAD_SIZE)
+
+        def head_step(h, cols):
             scores = lax.dot_general(
                 q_ref[0, :, cols], keys, (((1,), (1,)), ((), ())),
                 preferred_element_type=jnp.float32)
@@ -71,6 +71,16 @@
                 probs.astype(jnp.bfloat16), values, (((1,), (0,)), ((), ())),
                 preferred_element_type=jnp.float32)
             peak_sc[h] = peak_new
+
+        if masked:
+            def body(h, carry):
+                head_step(h, pl.ds(pl.multiple_of(h * HEAD_SIZE, HEAD_SIZE), HEAD_SIZE))
+                return carry
+
+            lax.fori_loop(0, heads, body, 0)
+        else:
+            for h in range(heads):
+                head_step(h, slice(h * HEAD_SIZE, (h + 1) * HEAD_SIZE))
 
     @pl.when(live & inner)
     def _():
@@ -200,7 +210,7 @@
     state = attend(queries, near_kv, near_meta, lo, query_pos.reshape(query_count, 1), None,
                    near_kv.shape[1] // key_tile)
     return attend(queries, kv, far_meta, lo, far_hi.reshape(query_count, 1), state,
-                  (LONGEST + query_count - 2) // key_tile + 2)
+                  max(1, (LONGEST - 1 - NEAR_BLOCKS * query_count) // key_tile + 2))
 
 
 def solution(mesh):

time: 223 us -> 238 us (1.067)
  Pallas kernels: 120 us -> 147 us
  waiting for transfers between devices: 47.6 us -> 35.6 us
    all_gather x1, waiting for transfers between devices: 44.2 us -> 0.01 us  [layer(): kv = lax.all_gather(local_kv, 'ctx', axis=1, tiled=True)]
    ppermute x3 -> x7, waiting for transfers between devices: 3.37 us -> 35.6 us  [layer(): lax.ppermute(local_kv, 'ctx', [(i, i + k) for i in range(ctx_size - k)])]
    pallas_call x2, Pallas kernels: 120 us -> 147 us  [attend(): pl.pallas_call(kernel, out_shape=out_shape, grid_spec=pltpu.PrefetchScala...]
    ppermute x3 -> x7, starting transfers between devices: 10 us -> 10.4 us  [layer(): lax.ppermute(local_kv, 'ctx', [(i, i + k) for i in range(ctx_size - k)])]
  transfers between devices with their start and end apart: 4 -> 8, of which waited for: 2 -> 4; matrix products, arithmetic and copies ran while one was open for 4% -> 3% of each run, Pallas kernels for 13% -> 25%
where the time goes in v2:
time: 238 us
  Pallas kernels  147 us (62%)
  waiting for transfers between devices  35.6 us (15%)
  between operations  17.7 us (7%)
  local copies, waits for them, and re-layouts  14 us (6%)
  blocking collectives  10.8 us (5%)
  starting transfers between devices  10.4 us (4%)
    pallas_call x2, Pallas kernels, attend(): pl.pallas_call(kernel, out_shape=out_shape, grid_spec=pltpu.PrefetchScala...  147 us
    ppermute x7, waiting for transfers between devices, layer(): lax.ppermute(local_kv, 'ctx', [(i, i + k) for i in range(ctx_size - k)])  35.6 us
    all_to_all x1, blocking collectives, layer(): lax.all_to_all(paired, 'head', split_axis=2, concat_axis=1, tiled=True)  10.8 us
    ppermute x7, starting transfers between devices, layer(): lax.ppermute(local_kv, 'ctx', [(i, i + k) for i in range(ctx_size - k)])  10.4 us
  transfers between devices with their start and end apart: 8, of which 4 were waited for; matrix products, arithmetic and copies ran while one was open for 3% of the time, Pallas kernels for 25%

profile of v2, /device:TPU:225, one launch (start us, length us, event | category | flops | bytes accessed | tf_op | source)
XLA Modules:
  0.0 237.7 jit_solution(871381621359741794)
XLA Ops:
  6.5 1.0 stack_reshape.8
  7.5 1.0 stack_reshape.9
  9.2 0.9 copy.28
  10.0 1.0 reshape.49
  11.0 10.8 %all_to_all.18 = bf16[8,2,8192]{2,1,0:T(2,128)(2,1)S(1)} all-to-all(bf16[8,2,8192]{2,1,0:T(2,128)(2,1)S(1)} %reshape.49), channel_id=1, replica_groups=mesh['ctx'=32,'head'=8] {'head'}, dimensions={0} | all-to-all | bytes 524288 | tf_op jit(solution)/shard_map/all_to_all | solution.py:174
  22.2 1.8 copy.30
  24.3 0.7 iota_add_fusion.hi_ref
  25.7 1.3 collective-permute-start
  27.1 1.3 collective-permute-start.1
  29.0 1.3 collective-permute-start.2
  34.9 0.8 copy.27.lo_ref
  36.3 1.9 stack.31.meta_ref
  38.1 1.9 stack.26.meta_ref
  40.1 1.3 collective-permute-start.3
  41.4 1.3 collective-permute-start.4
  42.7 10.8 %collective-permute-done = bf16[2,256,256]{2,1,0:T(8,128)(2,1)S(1)} collective-permute-done((bf16[2,256,256]{2,1,0:T(8,128)(2,1)}, bf16[2,256,256]{2,1,0:T(8,128)(2,1)S(1)}, u32[]{:S(2)}, u32[]{:S(2)}) %collective-permute-start) | collective-permute-done | bytes 262176 | tf_op jit(solution)/shard_map/ppermute | solution.py:179
  53.4 1.9 collective-permute-start.5
  55.4 10.1 %collective-permute-done.1 = bf16[2,256,256]{2,1,0:T(8,128)(2,1)S(1)} collective-permute-done((bf16[2,256,256]{2,1,0:T(8,128)(2,1)}, bf16[2,256,256]{2,1,0:T(8,128)(2,1)S(1)}, u32[]{:S(2)}, u32[]{:S(2)}) %collective-permute-start.1) | collective-permute-done | bytes 262176 | tf_op jit(solution)/shard_map/ppermute | solution.py:179
  65.5 2.1 collective-permute-start.6
  67.7 10.5 %collective-permute-done.4 = bf16[2,256,256]{2,1,0:T(8,128)(2,1)S(1)} collective-permute-done((bf16[2,256,256]{2,1,0:T(8,128)(2,1)}, bf16[2,256,256]{2,1,0:T(8,128)(2,1)S(1)}, u32[]{:S(2)}, u32[]{:S(2)}) %collective-permute-start.4) | collective-permute-done | bytes 262176 | tf_op jit(solution)/shard_map/ppermute | solution.py:179
  78.2 4.2 %collective-permute-done.5 = bf16[2,256,256]{2,1,0:T(8,128)(2,1)S(1)} collective-permute-done((bf16[2,256,256]{2,1,0:T(8,128)(2,1)}, bf16[2,256,256]{2,1,0:T(8,128)(2,1)S(1)}, u32[]{:S(2)}, u32[]{:S(2)}) %collective-permute-start.5) | collective-permute-done | bytes 262176 | tf_op jit(solution)/shard_map/ppermute | solution.py:179
  82.5 1.3 copy-done
  83.8 58.6 %shard_map.46 = (f32[2,16,256,128]{3,2,1,0:T(8,128)}, f32[2,16,256,128]{3,2,1,0:T(8,128)}, f32[2,16,256,128]{3,2,1,0:T(8,128)}) custom-call(s32[5]{0:T(128)} %stack.31.meta_ref, s32[256,1]{1,0:T(8,128)} %copy.27.lo_ref, s32[256,1]{1,0:T(8,128)} %iota_add_fusion.hi_ref, bf16[2,256,2048]{2,1,0:T(8,128)(2,1)} %q_ref.3, bf16[2,2048,256]{2,1,0:T(8,128)(2,1)} %copy-done, ...), custom_call_target="tpu_custom_call" | custom-call | tf_op jit(solution)/shard_map/pallas_call | solution.py:143
  142.4 88.5 %shard_map.47 = bf16[2,256,2048]{2,1,0:T(8,128)(2,1)} custom-call(s32[5]{0:T(128)} %stack.26.meta_ref, s32[256,1]{1,0:T(8,128)} %copy.27.lo_ref, s32[256,1]{1,0:T(8,128)} %broadcast_minimum_fusion.hi_ref, bf16[2,256,2048]{2,1,0:T(8,128)(2,1)} %q_ref.3, bf16[2,8192,256]{2,1,0:T(8,128)(2,1)} %all-gather.2.cloned.1.call-done.k_ref.v_ref, ...), custom_call_target="tpu_custom_call" | custom-call | tf_op jit(solution)/shard_map/pallas_call | solution.py:143
  (30 shorter events, 4.1 us)
Async XLA Ops:
  6.5 135.9 %all-gather.2.cloned.1.call-start = ((), (), s32[]{:S(2)}) async-start(), calls=%async_computation.1 | async-start | bytes 8650752 | tf_op jit(solution)/shard_map/all_gather | solution.py:185
  10.0 14.0 %copy-start.2 = (s32[16]{0:T(128)S(1)}, s32[16]{0:T(128)}, u32[]{:S(2)}) copy-start(s32[16]{0:T(128)} %param.4) | copy-start | bytes 196
  24.3 58.1 %copy-start.1 = (bf16[2,32,8,256]{3,1,2,0:T(8,128)(2,1)S(1)}, bf16[2,32,8,256]{3,1,2,0:T(8,128)(2,1)}, u32[]{:S(2)}) copy-start(bf16[2,32,8,256]{3,1,2,0:T(8,128)(2,1)} %copy.30) | copy-start | bytes 786436
  25.7 27.7 %collective-permute-start = (bf16[2,256,256]{2,1,0:T(8,128)(2,1)}, bf16[2,256,256]{2,1,0:T(8,128)(2,1)S(1)}, u32[]{:S(2)}, u32[]{:S(2)}) collective-permute-start(bf16[2,256,256]{2,1,0:T(8,128)(2,1)} %bitcast.20), channel_id=1, source_target_pairs={{0,56},{8,64},{16,72},{24,80},{32,88},{40,96},{48,104},{56,112},{6... | collective-permute-start | bytes 786440 | tf_op jit(solution)/shard_map/ppermute | solution.py:179
  27.1 38.4 %collective-permute-start.1 = (bf16[2,256,256]{2,1,0:T(8,128)(2,1)}, bf16[2,256,256]{2,1,0:T(8,128)(2,1)S(1)}, u32[]{:S(2)}, u32[]{:S(2)}) collective-permute-start(bf16[2,256,256]{2,1,0:T(8,128)(2,1)} %bitcast.21), channel_id=1, source_target_pairs={{0,48},{8,56},{16,64},{24,72},{32,80},{40,88},{48,96},{56,104},{64... | collective-permute-start | bytes 786440 | tf_op jit(solution)/shard_map/ppermute | solution.py:179
  29.0 38.6 %collective-permute-start.2 = (bf16[2,256,256]{2,1,0:T(8,128)(2,1)}, bf16[2,256,256]{2,1,0:T(8,128)(2,1)S(1)}, u32[]{:S(2)}, u32[]{:S(2)}) collective-permute-start(bf16[2,256,256]{2,1,0:T(8,128)(2,1)} %bitcast.22), channel_id=1, source_target_pairs={{0,40},{8,48},{16,56},{24,64},{32,72},{40,80},{48,88},{56,96},{64,... | collective-permute-start | bytes 786440 | tf_op jit(solution)/shard_map/ppermute | solution.py:179
  40.1 27.6 %collective-permute-start.3 = (bf16[2,256,256]{2,1,0:T(8,128)(2,1)}, bf16[2,256,256]{2,1,0:T(8,128)(2,1)S(1)}, u32[]{:S(2)}, u32[]{:S(2)}) collective-permute-start(bf16[2,256,256]{2,1,0:T(8,128)(2,1)} %bitcast.23), channel_id=1, source_target_pairs={{0,32},{8,40},{16,48},{24,56},{32,64},{40,72},{48,80},{56,88},{64,... | collective-permute-start | bytes 786440 | tf_op jit(solution)/shard_map/ppermute | solution.py:179
  41.4 36.9 %collective-permute-start.4 = (bf16[2,256,256]{2,1,0:T(8,128)(2,1)}, bf16[2,256,256]{2,1,0:T(8,128)(2,1)S(1)}, u32[]{:S(2)}, u32[]{:S(2)}) collective-permute-start(bf16[2,256,256]{2,1,0:T(8,128)(2,1)} %bitcast.24), channel_id=1, source_target_pairs={{0,24},{8,32},{16,40},{24,48},{32,56},{40,64},{48,72},{56,80},{64,... | collective-permute-start | bytes 786440 | tf_op jit(solution)/shard_map/ppermute | solution.py:179
  53.4 29.0 %collective-permute-start.5 = (bf16[2,256,256]{2,1,0:T(8,128)(2,1)}, bf16[2,256,256]{2,1,0:T(8,128)(2,1)S(1)}, u32[]{:S(2)}, u32[]{:S(2)}) collective-permute-start(bf16[2,256,256]{2,1,0:T(8,128)(2,1)} %bitcast.25), channel_id=1, source_target_pairs={{0,16},{8,24},{16,32},{24,40},{32,48},{40,56},{48,64},{56,72},{64,... | collective-permute-start | bytes 786440 | tf_op jit(solution)/shard_map/ppermute | solution.py:179
  65.5 16.9 %collective-permute-start.6 = (bf16[2,256,256]{2,1,0:T(8,128)(2,1)}, bf16[2,256,256]{2,1,0:T(8,128)(2,1)S(1)}, u32[]{:S(2)}, u32[]{:S(2)}) collective-permute-start(bf16[2,256,256]{2,1,0:T(8,128)(2,1)} %bitcast.26), channel_id=1, source_target_pairs={{0,8},{8,16},{16,24},{24,32},{32,40},{40,48},{48,56},{56,64},{64,7... | collective-permute-start | bytes 786440 | tf_op jit(solution)/shard_map/ppermute | solution.py:179
  82.5 1.3 copy-start
Sparse Core Ops, SparseCore 0:
  24.2 116.3 all-gather.1

commit v3 on v1

--- a/solution.py
+++ b/solution.py
@@ -15,7 +15,7 @@
 KEY_TILE = 512
 STAT_LANES = 128
 LOG2E = 1.4426950408889634
-NEAR_BLOCKS = 3
+NEAR_BLOCKS = 5
 
 
 def attend_kernel(meta_ref, lo_ref, hi_ref, q_ref, k_ref, v_ref, *rest,
@@ -63,8 +63,6 @@
             peak_new = jnp.maximum(peak_old, jnp.max(scores, axis=-1, keepdims=True))
             shift = peak_new * scale
             probs = jnp.exp2(scores * scale - jnp.tile(shift, (1, reps)))
-            if masked:
-                probs = jnp.where(allowed, probs, 0.0)
             factor = jnp.exp2(peak_old * scale - shift)
             total_sc[h] = total_sc[h] * factor + jnp.sum(probs, axis=-1, keepdims=True)
             accum_sc[h] = accum_sc[h] * factor + lax.dot_general(
@@ -200,7 +198,7 @@
     state = attend(queries, near_kv, near_meta, lo, query_pos.reshape(query_count, 1), None,
                    near_kv.shape[1] // key_tile)
     return attend(queries, kv, far_meta, lo, far_hi.reshape(query_count, 1), state,
-                  (LONGEST + query_count - 2) // key_tile + 2)
+                  max(1, (LONGEST - 1 - NEAR_BLOCKS * query_count) // key_tile + 2))
 
 
 def solution(mesh):

time: 223 us -> 208 us (0.933)
  the two profiles are of different devices: /device:TPU:225 before, /device:TPU:227 now
where the time goes in v3:
time: 208 us
  Pallas kernels  114 us (55%)
  waiting for transfers between devices  37.9 us (18%)
  between operations  17.4 us (8%)
  local copies, waits for them, and re-layouts  13.8 us (7%)
  starting transfers between devices  12.7 us (6%)
  blocking collectives  9.49 us (5%)
  other arithmetic  2.2 us (1%)
    pallas_call x2, Pallas kernels, attend(): pl.pallas_call(kernel, out_shape=out_shape, grid_spec=pltpu.PrefetchScala...  114 us
    ppermute x5, waiting for transfers between devices, layer(): lax.ppermute(local_kv, 'ctx', [(i, i + k) for i in range(ctx_size - k)])  20.1 us
    all_gather x1, waiting for transfers between devices, layer(): kv = lax.all_gather(local_kv, 'ctx', axis=1, tiled=True)  17.7 us
    ppermute x5, starting transfers between devices, layer(): lax.ppermute(local_kv, 'ctx', [(i, i + k) for i in range(ctx_size - k)])  12.7 us
    all_to_all x1, blocking collectives, layer(): lax.all_to_all(paired, 'head', split_axis=2, concat_axis=1, tiled=True)  9.49 us
  transfers between devices with their start and end apart: 6, of which 3 were waited for; matrix products, arithmetic and copies ran while one was open for 4% of the time, Pallas kernels for 19%

profile of v3, /device:TPU:227, one launch (start us, length us, event | category | flops | bytes accessed | tf_op | source)
XLA Modules:
  0.0 207.8 jit_solution(2066000165320904649)
XLA Ops:
  6.5 1.0 stack_reshape.8
  7.5 1.0 stack_reshape.9
  8.5 0.6 pad_maximum_fusion
  9.2 0.9 copy.28
  10.0 1.0 reshape.49
  11.0 9.5 %all_to_all.18 = bf16[8,2,8192]{2,1,0:T(2,128)(2,1)S(1)} all-to-all(bf16[8,2,8192]{2,1,0:T(2,128)(2,1)S(1)} %reshape.49), channel_id=1, replica_groups=mesh['ctx'=32,'head'=8] {'head'}, dimensions={0} | all-to-all | bytes 524288 | tf_op jit(solution)/shard_map/all_to_all | solution.py:162
  21.0 1.8 copy.30
  23.0 0.7 broadcast_minimum_fusion.hi_ref
  23.7 0.7 iota_add_fusion.hi_ref
  24.4 1.3 collective-permute-start
  25.8 1.3 collective-permute-start.1
  27.1 0.6 fusion
  27.7 1.3 collective-permute-start.2
  33.9 0.8 copy.27.lo_ref
  34.7 1.9 stack.31.meta_ref
  36.6 1.9 stack.26.meta_ref
  38.5 6.7 %collective-permute-start.4 = (bf16[2,256,256]{2,1,0:T(8,128)(2,1)}, bf16[2,256,256]{2,1,0:T(8,128)(2,1)S(1)}, u32[]{:S(2)}, u32[]{:S(2)}) collective-permute-start(bf16[2,256,256]{2,1,0:T(8,128)(2,1)} %bitcast.23), channel_id=1, source_target_pairs={{0,8},{8,16},{16,24},{24,32},{32,40},{40,48},{48,56},{56,64},{64,7... | collective-permute-start | bytes 786440 | tf_op jit(solution)/shard_map/ppermute | solution.py:167
  45.3 2.1 %collective-permute-start.3 = (bf16[2,256,256]{2,1,0:T(8,128)(2,1)}, bf16[2,256,256]{2,1,0:T(8,128)(2,1)S(1)}, u32[]{:S(2)}, u32[]{:S(2)}) collective-permute-start(bf16[2,256,256]{2,1,0:T(8,128)(2,1)} %bitcast.24), channel_id=1, source_target_pairs={{0,16},{8,24},{16,32},{24,40},{32,48},{40,56},{48,64},{56,72},{64,... | collective-permute-start | bytes 786440 | tf_op jit(solution)/shard_map/ppermute | solution.py:167
  47.5 13.3 %collective-permute-done.2 = bf16[2,256,256]{2,1,0:T(8,128)(2,1)S(1)} collective-permute-done((bf16[2,256,256]{2,1,0:T(8,128)(2,1)}, bf16[2,256,256]{2,1,0:T(8,128)(2,1)S(1)}, u32[]{:S(2)}, u32[]{:S(2)}) %collective-permute-start.2) | collective-permute-done | bytes 262176 | tf_op jit(solution)/shard_map/ppermute | solution.py:167
  60.8 6.8 %collective-permute-done.3 = bf16[2,256,256]{2,1,0:T(8,128)(2,1)S(1)} collective-permute-done((bf16[2,256,256]{2,1,0:T(8,128)(2,1)}, bf16[2,256,256]{2,1,0:T(8,128)(2,1)S(1)}, u32[]{:S(2)}, u32[]{:S(2)}) %collective-permute-start.3) | collective-permute-done | bytes 262176 | tf_op jit(solution)/shard_map/ppermute | solution.py:167
  67.7 1.1 copy-done
  68.9 39.0 %shard_map.46 = (f32[2,16,256,128]{3,2,1,0:T(8,128)}, f32[2,16,256,128]{3,2,1,0:T(8,128)}, f32[2,16,256,128]{3,2,1,0:T(8,128)}) custom-call(s32[5]{0:T(128)} %stack.31.meta_ref, s32[256,1]{1,0:T(8,128)} %copy.27.lo_ref, s32[256,1]{1,0:T(8,128)} %iota_add_fusion.hi_ref, bf16[2,256,2048]{2,1,0:T(8,128)(2,1)} %q_ref.3, bf16[2,1536,256]{2,1,0:T(8,128)(2,1)} %copy-done, ...), custom_call_target="tpu_custom_call" | custom-call | tf_op jit(solution)/shard_map/pallas_call | solution.py:131
  107.9 17.7 %all-gather.2.cloned.1.call-done.k_ref.v_ref = bf16[2,8192,256]{2,1,0:T(8,128)(2,1)} async-done(((bf16[2,256,256]{2,1,0:T(8,128)(2,1)}), bf16[2,8192,256]{2,1,0:T(8,128)(2,1)}) %all-gather.2.cloned.1.call-update) | async-done | bytes 8388624 | tf_op jit(solution)/shard_map/all_gather | solution.py:173
  125.6 75.3 %shard_map.47 = bf16[2,256,2048]{2,1,0:T(8,128)(2,1)} custom-call(s32[5]{0:T(128)} %stack.26.meta_ref, s32[256,1]{1,0:T(8,128)} %copy.27.lo_ref, s32[256,1]{1,0:T(8,128)} %broadcast_minimum_fusion.hi_ref, bf16[2,256,2048]{2,1,0:T(8,128)(2,1)} %q_ref.3, bf16[2,8192,256]{2,1,0:T(8,128)(2,1)} %all-gather.2.cloned.1.call-done.k_ref.v_ref, ...), custom_call_target="tpu_custom_call" | custom-call | tf_op jit(solution)/shard_map/pallas_call | solution.py:131
  (24 shorter events, 2.1 us)
Async XLA Ops:
  6.5 119.1 %all-gather.2.cloned.1.call-start = ((), (), s32[]{:S(2)}) async-start(), calls=%async_computation.1 | async-start | bytes 8650752 | tf_op jit(solution)/shard_map/all_gather | solution.py:173
  20.5 2.3 %copy-start.2 = (s32[16]{0:T(128)S(1)}, s32[16]{0:T(128)}, u32[]{:S(2)}) copy-start(s32[16]{0:T(128)} %param.4) | copy-start | bytes 196
  23.0 44.6 %copy-start.1 = (bf16[2,32,8,256]{3,1,2,0:T(8,128)(2,1)S(1)}, bf16[2,32,8,256]{3,1,2,0:T(8,128)(2,1)}, u32[]{:S(2)}) copy-start(bf16[2,32,8,256]{3,1,2,0:T(8,128)(2,1)} %copy.30) | copy-start | bytes 786436
  24.4 23.0 %collective-permute-start = (bf16[2,256,256]{2,1,0:T(8,128)(2,1)}, bf16[2,256,256]{2,1,0:T(8,128)(2,1)S(1)}, u32[]{:S(2)}, u32[]{:S(2)}) collective-permute-start(bf16[2,256,256]{2,1,0:T(8,128)(2,1)} %bitcast.20), channel_id=1, source_target_pairs={{0,40},{8,48},{16,56},{24,64},{32,72},{40,80},{48,88},{56,96},{64,... | collective-permute-start | bytes 786440 | tf_op jit(solution)/shard_map/ppermute | solution.py:167
  25.8 21.7 %collective-permute-start.1 = (bf16[2,256,256]{2,1,0:T(8,128)(2,1)}, bf16[2,256,256]{2,1,0:T(8,128)(2,1)S(1)}, u32[]{:S(2)}, u32[]{:S(2)}) collective-permute-start(bf16[2,256,256]{2,1,0:T(8,128)(2,1)} %bitcast.21), channel_id=1, source_target_pairs={{0,32},{8,40},{16,48},{24,56},{32,64},{40,72},{48,80},{56,88},{64,... | collective-permute-start | bytes 786440 | tf_op jit(solution)/shard_map/ppermute | solution.py:167
  27.7 33.1 %collective-permute-start.2 = (bf16[2,256,256]{2,1,0:T(8,128)(2,1)}, bf16[2,256,256]{2,1,0:T(8,128)(2,1)S(1)}, u32[]{:S(2)}, u32[]{:S(2)}) collective-permute-start(bf16[2,256,256]{2,1,0:T(8,128)(2,1)} %bitcast.22), channel_id=1, source_target_pairs={{0,24},{8,32},{16,40},{24,48},{32,56},{40,64},{48,72},{56,80},{64,... | collective-permute-start | bytes 786440 | tf_op jit(solution)/shard_map/ppermute | solution.py:167
  38.5 29.1 %collective-permute-start.4 = (bf16[2,256,256]{2,1,0:T(8,128)(2,1)}, bf16[2,256,256]{2,1,0:T(8,128)(2,1)S(1)}, u32[]{:S(2)}, u32[]{:S(2)}) collective-permute-start(bf16[2,256,256]{2,1,0:T(8,128)(2,1)} %bitcast.23), channel_id=1, source_target_pairs={{0,8},{8,16},{16,24},{24,32},{32,40},{40,48},{48,56},{56,64},{64,7... | collective-permute-start | bytes 786440 | tf_op jit(solution)/shard_map/ppermute | solution.py:167
  45.3 22.3 %collective-permute-start.3 = (bf16[2,256,256]{2,1,0:T(8,128)(2,1)}, bf16[2,256,256]{2,1,0:T(8,128)(2,1)S(1)}, u32[]{:S(2)}, u32[]{:S(2)}) collective-permute-start(bf16[2,256,256]{2,1,0:T(8,128)(2,1)} %bitcast.24), channel_id=1, source_target_pairs={{0,16},{8,24},{16,32},{24,40},{32,48},{40,56},{48,64},{56,72},{64,... | collective-permute-start | bytes 786440 | tf_op jit(solution)/shard_map/ppermute | solution.py:167
  67.7 1.1 copy-start
Sparse Core Ops, SparseCore 0:
  22.9 102.6 all-gather.1
